TPU v7x, 512 devices: a whole 4x4x16 slice. The times are simulated.
512 devices in a mesh: dp: 64 (over z, y), fsdp: 8 (over x, core).
Axes of the slice: x: 4, y: 4, z: 16, core: 2. Of those that a mesh axis runs over, the one named last changes fastest.
Arguments:
- tokens: bfloat16 [65536, 2048], P('dp', 'fsdp'), may hold values from -6 to 6
- norm_gain: bfloat16 [2048], replicated, may hold values from 0.25 to 1.75
- query_gain: bfloat16 [128], replicated, as said below
- key_gain: bfloat16 [128], replicated, as said below
- w_query: bfloat16 [2048, 2048], P('dp', 'fsdp'), as said below
- w_key: bfloat16 [2048, 1024], P('dp', 'fsdp'), as said below
- w_value: bfloat16 [2048, 1024], P('dp', 'fsdp'), may hold values from -0.125 to 0.125
- w_out: bfloat16 [2048, 2048], P('dp', 'fsdp'), may hold values from -0.125 to 0.125
- prompt_lengths: int32 [64, 8], replicated, may hold values from 1 to 512, 1024 in all within a row
- span_group: int32 [64, 64], replicated, may hold values from 0 to 63, as said below
Outputs:
- attention_update: bfloat16 [65536, 2048], P('dp', 'fsdp')
- kv_cache: bfloat16 [65536, 8, 256], P('dp', 'fsdp')
Inputs may be any that keep to these rules, and one draw needn't show every extreme that they name: `prompt_lengths`: row g sums to 1024. `span_group`: row i names, in arrival order, the group of each of its 64 blocks of 16 rows; every group is named exactly 64 times in all; every row names exactly one group twice and leaves exactly one group out, and every group is the one named twice by exactly one row. `query_gain`: Positive. `key_gain`: Positive. `w_query`: entries of size about one over the square root of 2048. `w_key`: entries of size about one over the square root of 2048.
All inputs are finite; a program needn't handle non-finite values.
Results may differ from a plain program's by a relative error of at most 0.0075.
The roundings to bfloat16 on the way count: a program that leaves them out, or rounds other values in their place, can miss the bound.
Values may be sent and summed in bfloat16 or wider, within the bound.
No kernel may reach another device: no remote copies, remote signals or barrier semaphores. Data moves between devices by JAX's collectives and lax.ppermute only.
A program may use at most 64 MiB of HBM per device.

v0:
```python
import math
import jax
import jax.numpy as jnp
from jax import lax
from jax.sharding import Mesh, PartitionSpec as P

QH = 16
KVH = 8
HD = 128
DP = ("z_hi", "z_lo", "y")
epsilon = 1e-06
rope_base = 1000000.0


def for_sending(x):

    def short(part):
        return part.astype(jnp.bfloat16) if part.dtype == jnp.float32 else part

    return jax.tree.map(short, x)


def head_norm(inputs, gains):
    inv_rms = lax.rsqrt(jnp.mean(inputs * inputs, axis=-1, keepdims=True) + epsilon)
    return inputs * inv_rms * gains.astype(jnp.float32)


def rotate(inputs, offsets):
    half_dim = inputs.shape[-1] // 2
    frequency = jnp.power(
        rope_base, -2.0 * jnp.arange(half_dim, dtype=jnp.float32) / inputs.shape[-1]
    )
    angles = offsets.astype(jnp.float32)[:, None] * frequency[None, :]
    cosine = jnp.cos(angles)[:, None, :]
    sine_part = jnp.sin(angles)[:, None, :]
    first_half = inputs[..., :half_dim]
    second = inputs[..., half_dim:]
    return jnp.concatenate(
        [first_half * cosine - second * sine_part, second * cosine + first_half * sine_part],
        axis=-1,
    )


def prompt_layout(lengths, group_rows):
    prompt_end = jnp.cumsum(lengths)
    begins = prompt_end - lengths
    position = jnp.arange(group_rows, dtype=jnp.int32)
    inside = (position[:, None] >= begins[None, :]) & (position[:, None] < prompt_end[None, :])
    starts = jnp.sum(jnp.where(inside, begins[None, :], 0), axis=1)
    return (position, starts)


def attend(query_block, key_rot, value_rows, pos_block, start_block, position):
    scores = jnp.einsum(
        "qkrd,skd->krqs", query_block, key_rot, preferred_element_type=jnp.float32
    ) * (1.0 / math.sqrt(HD))
    allowed = (position[None, :] <= pos_block[:, None]) & (
        position[None, :] >= start_block[:, None]
    )
    masked = jnp.where(allowed[None, None], scores, -jnp.inf)
    row_max = jnp.max(masked, axis=-1, keepdims=True)
    exp_scores = jnp.exp(masked - row_max)
    probs = (exp_scores / jnp.sum(exp_scores, axis=-1, keepdims=True)).astype(jnp.bfloat16)
    return jnp.einsum(
        "krqs,skd->qkrd", probs, value_rows, preferred_element_type=jnp.float32
    ).astype(jnp.bfloat16)


def local(
    tokens,
    norm_gain,
    query_gain,
    key_gain,
    w_query,
    w_key,
    w_value,
    w_out,
    prompt_lengths,
    span_group,
):
    group_rows, width_local = tokens.shape
    groups = lax.axis_size(DP)
    arrival_rows = group_rows // groups
    device_index = lax.axis_index(DP)
    block_ids = jnp.arange(groups, dtype=jnp.int32)
    own_blocks = lax.dynamic_index_in_dim(span_group, device_index, 0, keepdims=False)
    same = own_blocks[:, None] == own_blocks[None, :]
    dup_rank = jnp.sum(same & (block_ids[None, :] < block_ids[:, None]), axis=1).astype(jnp.int32)
    first_dest = jnp.where(dup_rank == 0, own_blocks, groups)
    slot_source = jnp.zeros((groups,), jnp.int32).at[first_dest].set(block_ids, mode="drop")
    dup_block = jnp.sum(jnp.where(dup_rank == 1, block_ids, 0))
    token_blocks = tokens.reshape(groups, arrival_rows, width_local)
    dup_tokens = lax.dynamic_index_in_dim(token_blocks, dup_block, 0, keepdims=False)
    weights = jnp.concatenate([w_query, w_key, w_value, w_out], axis=1)
    weight_rows, weight_width = weights.shape
    packed = jnp.concatenate([weights, dup_tokens.reshape(weight_rows, -1)], axis=1)
    packed = lax.all_gather(packed, "y", axis=0, tiled=True)
    packed, token_blocks = lax.optimization_barrier((packed, token_blocks))
    packed = lax.all_gather(packed, "z_lo", axis=0, tiled=True)
    packed = lax.all_gather(packed, "z_hi", axis=0, tiled=True)
    weights = packed[:, :weight_width]
    dup_all = packed[:, weight_width:].reshape(groups, arrival_rows, width_local)
    outgoing = jnp.take(token_blocks, slot_source, axis=0, mode="clip")
    incoming = lax.all_to_all(outgoing, DP, split_axis=0, concat_axis=0, tiled=True)
    counts = jnp.sum((span_group == device_index).astype(jnp.int32), axis=1)
    offsets = jnp.cumsum(counts) - counts
    first_pos = jnp.where(counts >= 1, offsets, groups)
    second_pos = jnp.where(counts == 2, offsets + 1, groups)
    source_of = (
        jnp.zeros((groups,), jnp.int32)
        .at[first_pos]
        .set(block_ids, mode="drop")
        .at[second_pos]
        .set(block_ids + groups, mode="drop")
    )
    pool = jnp.concatenate([incoming, dup_all], axis=0)
    arrived = jnp.take(pool, source_of, axis=0, mode="clip").reshape(group_rows, width_local)
    arrived, weights = lax.optimization_barrier((arrived, weights))
    full_rows = lax.all_gather(arrived, "fsdp", axis=1, tiled=True)
    cuts = [w_query.shape[1], w_key.shape[1], w_value.shape[1], w_out.shape[1]]
    bounds = [sum(cuts[:k]) for k in range(5)]
    query_full, key_full, value_full, out_full = (
        weights[:, bounds[k] : bounds[k + 1]] for k in range(4)
    )
    lengths = lax.dynamic_index_in_dim(prompt_lengths, device_index, 0, keepdims=False)
    position, starts = prompt_layout(lengths, group_rows)
    within = position - starts
    floats = full_rows.astype(jnp.float32)
    normed = (
        floats
        * lax.rsqrt(jnp.mean(floats * floats, axis=-1, keepdims=True) + epsilon)
        * norm_gain.astype(jnp.float32)
    ).astype(jnp.bfloat16)
    query = jnp.dot(normed, query_full, preferred_element_type=jnp.float32).reshape(
        group_rows, -1, HD
    )
    key_rows = jnp.dot(normed, key_full, preferred_element_type=jnp.float32).reshape(
        group_rows, -1, HD
    )
    value_rows = (
        jnp.dot(normed, value_full, preferred_element_type=jnp.float32)
        .reshape(group_rows, -1, HD)
        .astype(jnp.bfloat16)
    )
    query_rot = rotate(head_norm(query, query_gain), within).astype(jnp.bfloat16)
    key_rot = rotate(head_norm(key_rows, key_gain), within).astype(jnp.bfloat16)
    kv_heads = key_rot.shape[1]
    group_ratio = QH // KVH
    cache_rows = jnp.concatenate([key_rot, value_rows], axis=-1)
    block_count = group_rows // 512
    block_len = group_rows // block_count
    query_heads = query_rot.reshape(block_count, block_len, kv_heads, group_ratio, HD)

    def one_block(pieces):
        query_block, pos_block, start_block = pieces
        return attend(query_block, key_rot, value_rows, pos_block, start_block, position)

    mixed = lax.map(
        one_block,
        (
            query_heads,
            position.reshape(block_count, block_len),
            starts.reshape(block_count, block_len),
        ),
    )
    mixed = mixed.reshape(group_rows, kv_heads * group_ratio * HD)
    heads_all = lax.all_gather(mixed, "fsdp", axis=1, tiled=True)
    update = jnp.dot(heads_all, out_full, preferred_element_type=jnp.float32).astype(jnp.bfloat16)
    cache_flat = cache_rows.reshape(group_rows, -1)
    update_width = update.shape[1]
    joined = jnp.concatenate([update, cache_flat], axis=1).reshape(groups, arrival_rows, -1)
    sent = jnp.take(joined, offsets, axis=0, mode="clip")
    dup_position = jnp.sum(jnp.where(counts == 2, offsets + 1, 0))
    dup_result = lax.dynamic_index_in_dim(joined, dup_position, 0, keepdims=True)
    dup_result = lax.all_gather(dup_result, "y", axis=0, tiled=True)
    dup_result = lax.all_gather(dup_result, "z_lo", axis=0, tiled=True)
    dup_result = lax.all_gather(dup_result, "z_hi", axis=0, tiled=True)
    back = lax.all_to_all(sent, DP, split_axis=0, concat_axis=0, tiled=True)
    pool_back = jnp.concatenate([back, dup_result], axis=0)
    mine = jnp.take(pool_back, own_blocks + groups * dup_rank, axis=0, mode="clip").reshape(
        group_rows, -1
    )
    attention_out = mine[:, :update_width]
    cache_out = mine[:, update_width:].reshape(cache_rows.shape)
    return (attention_out, cache_out)


def solution(mesh):
    z_size = mesh.shape["dp"] // 4
    fine = Mesh(
        mesh.devices.reshape(z_size // 4, 4, 4, mesh.shape["fsdp"]), ("z_hi", "z_lo", "y", "fsdp")
    )
    return jax.shard_map(
        local,
        mesh=fine,
        in_specs=(
            P(DP, "fsdp"),
            P(),
            P(),
            P(),
            P(DP, "fsdp"),
            P(DP, "fsdp"),
            P(DP, "fsdp"),
            P(DP, "fsdp"),
            P(),
            P(),
        ),
        out_specs=(P(DP, "fsdp"), P(DP, "fsdp", None)),
        check_vma=False,
    )
```

profile of v0, /device:TPU:1, one launch (start us, length us, event | category | flops | bytes accessed | tf_op | source)
XLA Modules:
  0.0 475.8 jit_solution(10181882392468857005)
XLA Ops:
  13.6 10.6 %all_gather.24 = bf16[128,896]{1,0:T(8,128)(2,1)S(1)} all-gather(bf16[32,896]{1,0:T(8,128)(2,1)S(1)} %constant_dynamic-update-slice_fusion), channel_id=1, replica_groups=mesh['z_hi'=4,'z_lo'=4,'y'=4,'fsdp'=8] {'y'}, dimensions={0}, use_global_device_ids=true | all-gather | bytes 286720 | tf_op jit(solution)/shard_map/all_gather | solution.py:97
  24.3 18.4 %all_gather.25 = bf16[512,896]{1,0:T(8,128)(2,1)} all-gather(bf16[128,896]{1,0:T(8,128)(2,1)S(1)} %all_gather.24), channel_id=1, replica_groups=mesh['z_hi'=4,'z_lo'=4,'y'=4,'fsdp'=8] {'z_lo'}, dimensions={0}, use_global_device_ids=true | all-gather | bytes 1146880 | tf_op jit(solution)/shard_map/all_gather | solution.py:99
  45.8 1.4 gather_fusion
  47.1 16.7 %all-to-all-start = ((bf16[64,16,256]{2,1,0:T(8,128)(2,1)}), bf16[64,16,256]{2,1,0:T(8,128)(2,1)S(1)}, u32[]{:S(2)}, u32[]{:S(2)}) async-start(bf16[64,16,256]{2,1,0:T(8,128)(2,1)} %gather_fusion), calls=%async_computation | async-start | bytes 1048576 | tf_op jit(solution)/shard_map/all_to_all | solution.py:104
  65.5 145.7 %all-gather.5.cloned.1.call-done = bf16[2048,896]{1,0:T(8,128)(2,1)} async-done(((bf16[512,896]{1,0:T(8,128)(2,1)}), bf16[2048,896]{1,0:T(8,128)(2,1)}) %all-gather.5.cloned.1.call-update) | async-done | bytes 3670032 | tf_op jit(solution)/shard_map/all_gather | solution.py:100
  211.2 1.1 slice.56
  212.7 1.4 gather_fusion.1
  214.1 3.8 slice.57
  219.4 37.9 %all-gather.7.cloned.1.call-done = bf16[1024,2048]{1,0:T(8,128)(2,1)} async-done(((bf16[1024,256]{1,0:T(8,128)(2,1)}), bf16[1024,2048]{1,0:T(8,128)(2,1)}) %all-gather.7.cloned.1.call-update) | async-done | bytes 4194320 | tf_op jit(solution)/shard_map/all_gather | solution.py:119
  257.3 3.2 fusion.21
  260.8 1.0 fusion.23
  262.7 1.5 multiply_reduce_fusion.1
  264.2 1.3 multiply_reduce_fusion
  265.5 1.2 convolution_convert_fusion.1
  266.9 1.3 fusion.35
  271.1 9.4 %while.12 = (s32[]{:T(128)}, bf16[2,512,1,2,128]{4,3,1,0,2:T(2,128)(2,1)S(1)}, s32[2,512]{1,0:T(2,128)S(1)}, s32[2,512]{1,0:T(2,128)S(1)}, bf16[2,512,1,2,128]{4...) while((s32[]{:T(128)}, ...), condition=%wide.region_15.16_spmd.clone.clone, body=%wide.region_12.15_spmd.clone.clone.sunk | while | flops 551155712 | bytes 16285793 | solution.py:158
  271.7 1.0 fusion.67
  272.8 1.2 fusion.68
  273.9 1.6 fusion.69
  276.4 1.0 fusion.67
  277.5 1.2 fusion.68
  278.7 1.6 fusion.69
  281.8 44.0 %all-gather.9.cloned.1.call-done = bf16[1024,2048]{1,0:T(8,128)(2,1)} async-done(((bf16[1024,256]{1,0:T(8,128)(2,1)}), bf16[1024,2048]{1,0:T(8,128)(2,1)}) %all-gather.9.cloned.1.call-update) | async-done | bytes 4194320 | tf_op jit(solution)/shard_map/all_gather | solution.py:167
  325.8 3.7 convolution_convert_fusion
  329.8 1.6 gather_fusion.2
  331.5 15.6 %all-to-all-start.1 = ((bf16[64,16,512]{2,1,0:T(8,128)(2,1)}), bf16[64,16,512]{2,1,0:T(8,128)(2,1)}, u32[]{:S(2)}, u32[]{:S(2)}) async-start(bf16[64,16,512]{2,1,0:T(8,128)(2,1)} %gather_fusion.2), calls=%async_computation.1 | async-start | bytes 2097152 | tf_op jit(solution)/shard_map/all_to_all | solution.py:178
  349.7 10.3 %all_gather.29 = bf16[4,16,512]{2,1,0:T(8,128)(2,1)S(1)} all-gather(bf16[1,16,512]{2,1,0:T(8,128)(2,1)S(1)} %constant_dynamic-slice_fusion.2), channel_id=1, replica_groups=mesh['z_hi'=4,'z_lo'=4,'y'=4,'fsdp'=8] {'y'}, dimensions={0}, use_global_device_ids=true | all-gather | bytes 81920 | tf_op jit(solution)/shard_map/all_gather | solution.py:175
  360.1 40.8 %all_gather.30 = bf16[16,16,512]{2,1,0:T(8,128)(2,1)} all-gather(bf16[4,16,512]{2,1,0:T(8,128)(2,1)S(1)} %all_gather.29), channel_id=1, replica_groups=mesh['z_hi'=4,'z_lo'=4,'y'=4,'fsdp'=8] {'z_lo'}, dimensions={0}, use_global_device_ids=true | all-gather | bytes 327680 | tf_op jit(solution)/shard_map/all_gather | solution.py:176
  400.9 62.8 %all-gather.11.cloned.1.call-done = bf16[64,16,512]{2,1,0:T(8,128)(2,1)} async-done(((bf16[16,16,512]{2,1,0:T(8,128)(2,1)}), bf16[64,16,512]{2,1,0:T(8,128)(2,1)}) %all-gather.11.cloned.1.call-update) | async-done | bytes 1048592 | tf_op jit(solution)/shard_map/all_gather | solution.py:177
  463.7 1.7 pad_maximum_fusion
  465.4 1.6 gather_fusion.3
  467.0 2.2 slice_bitcast_fusion
  (94 shorter events, 18.9 us)
Async XLA Ops:
  7.2 3.6 copy-start
  7.2 204.1 %all-gather.5.cloned.1.call-start = ((), (), s32[]{:S(2)}) async-start(), calls=%async_computation.2 | async-start | bytes 4587520 | tf_op jit(solution)/shard_map/all_gather | solution.py:100
  47.1 165.4 %all-to-all-start = ((bf16[64,16,256]{2,1,0:T(8,128)(2,1)}), bf16[64,16,256]{2,1,0:T(8,128)(2,1)S(1)}, u32[]{:S(2)}, u32[]{:S(2)}) async-start(bf16[64,16,256]{2,1,0:T(8,128)(2,1)} %gather_fusion), calls=%async_computation | async-start | bytes 1048576 | tf_op jit(solution)/shard_map/all_to_all | solution.py:104
  63.9 193.5 %all-gather.7.cloned.1.call-start = ((), (), s32[]{:S(2)}) async-start(), calls=%async_computation.3 | async-start | bytes 4718592 | tf_op jit(solution)/shard_map/all_gather | solution.py:119
  212.6 5.3 %copy-start.4 = (bf16[2048]{0:T(1024)(128)(2,1)S(1)}, bf16[2048]{0:T(1024)(128)(2,1)}, u32[]{:S(2)}) copy-start(bf16[2048]{0:T(1024)(128)(2,1)} %param.13) | copy-start | bytes 12292
  212.6 5.3 %copy-start.6 = (bf16[128]{0:T(256)(128)(2,1)S(1)}, bf16[128]{0:T(256)(128)(2,1)}, u32[]{:S(2)}) copy-start(bf16[128]{0:T(256)(128)(2,1)} %param.15) | copy-start | bytes 772
  212.6 5.3 %copy-start.5 = (s32[64,8]{0,1:T(8,128)S(1)}, s32[64,8]{0,1:T(8,128)}, u32[]{:S(2)}) copy-start(s32[64,8]{0,1:T(8,128)} %param.20) | copy-start | bytes 6148
  212.7 5.7 %copy-start.7 = (bf16[128]{0:T(256)(128)(2,1)S(1)}, bf16[128]{0:T(256)(128)(2,1)}, u32[]{:S(2)}) copy-start(bf16[128]{0:T(256)(128)(2,1)} %param.14) | copy-start | bytes 772
  217.8 107.9 %all-gather.9.cloned.1.call-start = ((), (), s32[]{:S(2)}) async-start(), calls=%async_computation.4 | async-start | bytes 4718592 | tf_op jit(solution)/shard_map/all_gather | solution.py:167
  257.3 3.4 copy-start.1
  260.8 1.9 copy-start.2
  269.3 1.7 copy-start.3
  331.5 132.2 %all-to-all-start.1 = ((bf16[64,16,512]{2,1,0:T(8,128)(2,1)}), bf16[64,16,512]{2,1,0:T(8,128)(2,1)}, u32[]{:S(2)}, u32[]{:S(2)}) async-start(bf16[64,16,512]{2,1,0:T(8,128)(2,1)} %gather_fusion.2), calls=%async_computation.1 | async-start | bytes 2097152 | tf_op jit(solution)/shard_map/all_to_all | solution.py:178
  347.1 116.6 %all-gather.11.cloned.1.call-start = ((), (), s32[]{:S(2)}) async-start(), calls=%async_computation.5 | async-start | bytes 1310720 | tf_op jit(solution)/shard_map/all_gather | solution.py:177
Sparse Core Ops, SparseCore 0:
  42.8 168.3 all-gather.4
  218.0 39.3 all-gather.6
  281.6 44.1 all-gather.8
  401.0 62.6 all-gather.10
where the time goes:
time: 477 us; the launch traced here: 476 us
  waiting for transfers between devices  290 us (61%)
  blocking collectives  80.1 us (17%)
  starting transfers between devices  32.5 us (7%)
  local copies, waits for them, and re-layouts  24.3 us (5%)
  between operations  18.1 us (4%)
  other arithmetic  17.1 us (4%)
  matrix products  13 us (3%)
    all_gather x1, waiting for transfers between devices, local(): packed = lax.all_gather(packed, 'z_hi', axis=0, tiled=True)  146 us
    all_gather x1, waiting for transfers between devices, local(): dup_result = lax.all_gather(dup_result, 'z_hi', axis=0, tiled=True)  62.8 us
    all_gather x1, waiting for transfers between devices, local(): heads_all = lax.all_gather(mixed, 'fsdp', axis=1, tiled=True)  44 us
    all_gather x1, blocking collectives, local(): dup_result = lax.all_gather(dup_result, 'z_lo', axis=0, tiled=True)  40.8 us
    all_gather x1, waiting for transfers between devices, local(): full_rows = lax.all_gather(arrived, 'fsdp', axis=1, tiled=True)  37.9 us
    all_gather x1, blocking collectives, local(): packed = lax.all_gather(packed, 'z_lo', axis=0, tiled=True)  18.4 us
    all_to_all x1, starting transfers between devices, local(): lax.all_to_all(outgoing, DP, split_axis=0, concat_axis=0, tiled=True)  16.7 us
    all_to_all x1, starting transfers between devices, local(): back = lax.all_to_all(sent, DP, split_axis=0, concat_axis=0, tiled=True)  15.6 us
  transfers between devices with their start and end apart: 6, of which 4 were waited for; matrix products, arithmetic and copies ran while one was open for 2% of the time, Pallas kernels for 0%

commit v1 on v0

--- a/solution.py
+++ b/solution.py
@@ -116,7 +116,9 @@
     pool = jnp.concatenate([incoming, dup_all], axis=0)
     arrived = jnp.take(pool, source_of, axis=0, mode="clip").reshape(group_rows, width_local)
     arrived, weights = lax.optimization_barrier((arrived, weights))
-    full_rows = lax.all_gather(arrived, "fsdp", axis=1, tiled=True)
+    full_rows = jnp.concatenate(
+        lax.all_to_all(jnp.stack([arrived] * lax.axis_size("fsdp")), "fsdp", 0, 0), axis=1
+    )
     cuts = [w_query.shape[1], w_key.shape[1], w_value.shape[1], w_out.shape[1]]
     bounds = [sum(cuts[:k]) for k in range(5)]
     query_full, key_full, value_full, out_full = (

time: 477 us -> 495 us (1.038)
  local copies, waits for them, and re-layouts: 24.3 us -> 32.8 us
  starting transfers between devices: 32.5 us -> 38 us
    all_to_all x0 -> x1, waiting for transfers between devices: none -> 45.3 us  [local(): lax.all_to_all(jnp.stack([arrived] * lax.axis_size('fsdp')), 'fsdp', 0, 0)]
    all_gather x1 -> x0, waiting for transfers between devices: 37.9 us -> none  [local(): full_rows = lax.all_gather(arrived, 'fsdp', axis=1, tiled=True)]
    all_gather x1, waiting for transfers between devices: 44 us -> 37.2 us  [local(): heads_all = lax.all_gather(mixed, 'fsdp', axis=1, tiled=True)]
    all_to_all x0 -> x1, local copies, waits for them, and re-layouts: none -> 6.45 us  [local(): lax.all_to_all(jnp.stack([arrived] * lax.axis_size('fsdp')), 'fsdp', 0, 0)]
    all_to_all x0 -> x1, starting transfers between devices: none -> 5.63 us  [local(): lax.all_to_all(jnp.stack([arrived] * lax.axis_size('fsdp')), 'fsdp', 0, 0)]
where the time goes in v1:
time: 495 us; the launch traced here: 493 us
  waiting for transfers between devices  291 us (59%)
  blocking collectives  80.1 us (16%)
  starting transfers between devices  38 us (8%)
  local copies, waits for them, and re-layouts  32.8 us (7%)
  between operations  18.1 us (4%)
  other arithmetic  17.7 us (4%)
  matrix products  15.1 us (3%)
    all_gather x1, waiting for transfers between devices, local(): packed = lax.all_gather(packed, 'z_hi', axis=0, tiled=True)  146 us
    all_gather x1, waiting for transfers between devices, local(): dup_result = lax.all_gather(dup_result, 'z_hi', axis=0, tiled=True)  62.8 us
    all_to_all x1, waiting for transfers between devices, local(): lax.all_to_all(jnp.stack([arrived] * lax.axis_size('fsdp')), 'fsdp', 0, 0)  45.3 us
    all_gather x1, blocking collectives, local(): dup_result = lax.all_gather(dup_result, 'z_lo', axis=0, tiled=True)  40.8 us
    all_gather x1, waiting for transfers between devices, local(): heads_all = lax.all_gather(mixed, 'fsdp', axis=1, tiled=True)  37.2 us
    all_gather x1, blocking collectives, local(): packed = lax.all_gather(packed, 'z_lo', axis=0, tiled=True)  18.4 us
    all_to_all x1, starting transfers between devices, local(): lax.all_to_all(outgoing, DP, split_axis=0, concat_axis=0, tiled=True)  16.7 us
    all_to_all x1, starting transfers between devices, local(): back = lax.all_to_all(sent, DP, split_axis=0, concat_axis=0, tiled=True)  15.6 us
  transfers between devices with their start and end apart: 6, of which 4 were waited for; matrix products, arithmetic and copies ran while one was open for 2% of the time, Pallas kernels for 0%

profile of v1, /device:TPU:1, one launch (start us, length us, event | category | flops | bytes accessed | tf_op | source)
XLA Modules:
  0.0 493.3 jit_solution(6548145580259808417)
XLA Ops:
  13.6 10.6 %all_gather.21 = bf16[128,896]{1,0:T(8,128)(2,1)S(1)} all-gather(bf16[32,896]{1,0:T(8,128)(2,1)S(1)} %constant_dynamic-update-slice_fusion), channel_id=1, replica_groups=mesh['z_hi'=4,'z_lo'=4,'y'=4,'fsdp'=8] {'y'}, dimensions={0}, use_global_device_ids=true | all-gather | bytes 286720 | tf_op jit(solution)/shard_map/all_gather | solution.py:97
  24.3 18.4 %all_gather.22 = bf16[512,896]{1,0:T(8,128)(2,1)} all-gather(bf16[128,896]{1,0:T(8,128)(2,1)S(1)} %all_gather.21), channel_id=1, replica_groups=mesh['z_hi'=4,'z_lo'=4,'y'=4,'fsdp'=8] {'z_lo'}, dimensions={0}, use_global_device_ids=true | all-gather | bytes 1146880 | tf_op jit(solution)/shard_map/all_gather | solution.py:99
  45.8 1.4 gather_fusion
  47.1 16.7 %all-to-all-start = ((bf16[64,16,256]{2,1,0:T(8,128)(2,1)}), bf16[64,16,256]{2,1,0:T(8,128)(2,1)S(1)}, u32[]{:S(2)}, u32[]{:S(2)}) async-start(bf16[64,16,256]{2,1,0:T(8,128)(2,1)} %gather_fusion), calls=%async_computation | async-start | bytes 1048576 | tf_op jit(solution)/shard_map/all_to_all | solution.py:104
  65.5 145.8 %all-gather.4.cloned.1.call-done = bf16[2048,896]{1,0:T(8,128)(2,1)} async-done(((bf16[512,896]{1,0:T(8,128)(2,1)}), bf16[2048,896]{1,0:T(8,128)(2,1)}) %all-gather.4.cloned.1.call-update) | async-done | bytes 3670032 | tf_op jit(solution)/shard_map/all_gather | solution.py:100
  213.2 3.8 slice.57
  217.1 2.2 stack.2
  219.3 5.6 %all-to-all-start.1 = ((bf16[8,1024,256]{2,1,0:T(8,128)(2,1)}), bf16[8,1024,256]{2,1,0:T(8,128)(2,1)}, u32[]{:S(2)}, u32[]{:S(2)}) async-start(bf16[8,1024,256]{2,1,0:T(8,128)(2,1)} %stack.2), calls=%async_computation.1 | async-start | bytes 8388608 | tf_op jit(solution)/shard_map/all_to_all | solution.py:120
  226.5 1.3 slice_bitcast_fusion
  228.5 45.3 %all-to-all-done.1 = bf16[8,1024,256]{2,1,0:T(8,128)(2,1)} async-done(((bf16[8,1024,256]{2,1,0:T(8,128)(2,1)}), bf16[8,1024,256]{2,1,0:T(8,128)(2,1)}, u32[]{:S(2)}, u32[]{:S(2)}) %all-to-all-start.1) | async-done | bytes 4194336 | tf_op jit(solution)/shard_map/all_to_all | solution.py:120
  273.7 6.5 %copy.76 = bf16[8,1024,256]{1,2,0:T(8,128)(2,1)} copy(bf16[8,1024,256]{2,1,0:T(8,128)(2,1)} %all-to-all-done.1) | data formatting | bytes 8388608 | tf_op jit(solution)/shard_map/all_to_all | solution.py:120
  280.2 3.3 multiply_reduce_fusion
  284.7 3.0 convolution_convert_fusion.1
  287.7 1.9 multiply_reduce_fusion.2
  289.7 1.2 fusion.32
  290.9 1.1 multiply_convert_fusion
  292.0 1.3 multiply_reduce_fusion.1
  295.2 9.7 %while.12 = (s32[]{:T(128)}, bf16[2,512,1,2,128]{4,3,1,0,2:T(2,128)(2,1)S(1)}, s32[2,512]{1,0:T(2,128)S(1)}, s32[2,512]{1,0:T(2,128)S(1)}, bf16[2,512,1,2,128]{4...) while((s32[]{:T(128)}, ...), condition=%wide.region_15.16_spmd.clone.clone, body=%wide.region_12.15_spmd.clone.clone.sunk | while | flops 551155712 | bytes 17334404 | solution.py:160
  297.1 1.2 fusion.66
  298.2 1.6 fusion.67
  301.8 1.2 fusion.66
  303.0 1.6 fusion.67
  306.1 37.2 %all-gather.6.cloned.1.call-done = bf16[1024,2048]{1,0:T(8,128)(2,1)} async-done(((bf16[1024,256]{1,0:T(8,128)(2,1)}), bf16[1024,2048]{1,0:T(8,128)(2,1)}) %all-gather.6.cloned.1.call-update) | async-done | bytes 4194320 | tf_op jit(solution)/shard_map/all_gather | solution.py:169
  343.3 3.7 convolution_convert_fusion
  347.4 1.6 gather_fusion.2
  349.0 15.6 %all-to-all-start.2 = ((bf16[64,16,512]{2,1,0:T(8,128)(2,1)}), bf16[64,16,512]{2,1,0:T(8,128)(2,1)}, u32[]{:S(2)}, u32[]{:S(2)}) async-start(bf16[64,16,512]{2,1,0:T(8,128)(2,1)} %gather_fusion.2), calls=%async_computation.2 | async-start | bytes 2097152 | tf_op jit(solution)/shard_map/all_to_all | solution.py:180
  367.3 10.3 %all_gather.25 = bf16[4,16,512]{2,1,0:T(8,128)(2,1)S(1)} all-gather(bf16[1,16,512]{2,1,0:T(8,128)(2,1)S(1)} %constant_dynamic-slice_fusion.2), channel_id=1, replica_groups=mesh['z_hi'=4,'z_lo'=4,'y'=4,'fsdp'=8] {'y'}, dimensions={0}, use_global_device_ids=true | all-gather | bytes 81920 | tf_op jit(solution)/shard_map/all_gather | solution.py:177
  377.6 40.8 %all_gather.26 = bf16[16,16,512]{2,1,0:T(8,128)(2,1)} all-gather(bf16[4,16,512]{2,1,0:T(8,128)(2,1)S(1)} %all_gather.25), channel_id=1, replica_groups=mesh['z_hi'=4,'z_lo'=4,'y'=4,'fsdp'=8] {'z_lo'}, dimensions={0}, use_global_device_ids=true | all-gather | bytes 327680 | tf_op jit(solution)/shard_map/all_gather | solution.py:178
  418.5 62.8 %all-gather.8.cloned.1.call-done = bf16[64,16,512]{2,1,0:T(8,128)(2,1)} async-done(((bf16[16,16,512]{2,1,0:T(8,128)(2,1)}), bf16[64,16,512]{2,1,0:T(8,128)(2,1)}) %all-gather.8.cloned.1.call-update) | async-done | bytes 1048592 | tf_op jit(solution)/shard_map/all_gather | solution.py:179
  481.2 1.7 pad_maximum_fusion
  483.0 1.6 gather_fusion.3
  484.6 2.2 slice_bitcast_fusion.1
  (104 shorter events, 22.4 us)
Async XLA Ops:
  7.2 4.3 copy-start
  7.2 204.1 %all-gather.4.cloned.1.call-start = ((), (), s32[]{:S(2)}) async-start(), calls=%async_computation.3 | async-start | bytes 4587520 | tf_op jit(solution)/shard_map/all_gather | solution.py:100
  47.1 165.4 %all-to-all-start = ((bf16[64,16,256]{2,1,0:T(8,128)(2,1)}), bf16[64,16,256]{2,1,0:T(8,128)(2,1)S(1)}, u32[]{:S(2)}, u32[]{:S(2)}) async-start(bf16[64,16,256]{2,1,0:T(8,128)(2,1)} %gather_fusion), calls=%async_computation | async-start | bytes 1048576 | tf_op jit(solution)/shard_map/all_to_all | solution.py:104
  219.3 5.6 %copy-start.5 = (bf16[2048]{0:T(1024)(128)(2,1)S(1)}, bf16[2048]{0:T(1024)(128)(2,1)}, u32[]{:S(2)}) copy-start(bf16[2048]{0:T(1024)(128)(2,1)} %param.13) | copy-start | bytes 12292
  219.3 5.7 %copy-start.7 = (bf16[128]{0:T(256)(128)(2,1)S(1)}, bf16[128]{0:T(256)(128)(2,1)}, u32[]{:S(2)}) copy-start(bf16[128]{0:T(256)(128)(2,1)} %param.15) | copy-start | bytes 772
  219.3 5.7 %copy-start.6 = (s32[64,8]{0,1:T(8,128)S(1)}, s32[64,8]{0,1:T(8,128)}, u32[]{:S(2)}) copy-start(s32[64,8]{0,1:T(8,128)} %param.20) | copy-start | bytes 6148
  219.3 6.2 %copy-start.8 = (bf16[128]{0:T(256)(128)(2,1)S(1)}, bf16[128]{0:T(256)(128)(2,1)}, u32[]{:S(2)}) copy-start(bf16[128]{0:T(256)(128)(2,1)} %param.14) | copy-start | bytes 772
  219.3 54.4 %all-to-all-start.1 = ((bf16[8,1024,256]{2,1,0:T(8,128)(2,1)}), bf16[8,1024,256]{2,1,0:T(8,128)(2,1)}, u32[]{:S(2)}, u32[]{:S(2)}) async-start(bf16[8,1024,256]{2,1,0:T(8,128)(2,1)} %stack.2), calls=%async_computation.1 | async-start | bytes 8388608 | tf_op jit(solution)/shard_map/all_to_all | solution.py:120
  224.9 118.4 %all-gather.6.cloned.1.call-start = ((), (), s32[]{:S(2)}) async-start(), calls=%async_computation.4 | async-start | bytes 4718592 | tf_op jit(solution)/shard_map/all_gather | solution.py:169
  280.2 3.4 copy-start.1
  293.5 1.7 copy-start.2
  296.0 2.2 copy-start.3
  300.8 2.2 copy-start.3
  306.0 41.1 %copy-start.4 = (bf16[1024,1,128]{2,0,1:T(8,128)(2,1)S(1)}, bf16[1024,1,128]{2,0,1:T(8,128)(2,1)}, u32[]{:S(2)}) copy-start(bf16[1024,1,128]{2,0,1:T(8,128)(2,1)} %get-tuple-element.254) | copy-start | bytes 786436
  349.0 132.2 %all-to-all-start.2 = ((bf16[64,16,512]{2,1,0:T(8,128)(2,1)}), bf16[64,16,512]{2,1,0:T(8,128)(2,1)}, u32[]{:S(2)}, u32[]{:S(2)}) async-start(bf16[64,16,512]{2,1,0:T(8,128)(2,1)} %gather_fusion.2), calls=%async_computation.2 | async-start | bytes 2097152 | tf_op jit(solution)/shard_map/all_to_all | solution.py:180
  364.7 116.6 %all-gather.8.cloned.1.call-start = ((), (), s32[]{:S(2)}) async-start(), calls=%async_computation.5 | async-start | bytes 1310720 | tf_op jit(solution)/shard_map/all_gather | solution.py:179
Sparse Core Ops, SparseCore 0:
  42.8 168.3 all-gather.3
  305.9 37.4 all-gather.5
  418.6 62.6 all-gather.7
